TPU v7x, 128 devices: a whole 4x4x4 slice. The times are simulated.
128 devices in a mesh: group: 16 (over x, z), mp: 8 (over y, core).
Axes of the slice: x: 4, y: 4, z: 4, core: 2. Of those that a mesh axis runs over, the one named last changes fastest.
Arguments:
- stream: bfloat16 [8192, 3584], P('group', 'mp'), may hold values from -6 to 6
- prenorm_gain: float32 [3584], replicated, may hold values from 0.25 to 12
- query_weight: bfloat16 [3584, 4096], P(None, 'mp'), may hold values from -0.09375 to 0.09375
- key_weight: bfloat16 [3584, 2048], P(None, 'mp'), may hold values from -0.09375 to 0.09375
- value_weight: bfloat16 [3584, 2048], P(None, 'mp'), may hold values from -0.09375 to 0.09375
- output_weight: bfloat16 [4096, 3584], P('mp'), may hold values from -0.09375 to 0.09375
- adapter_down_rows: bfloat16 [64, 16, 3584], P('group', None, 'mp'), may hold values from -0.09375 to 0.09375
- adapter_up_query: bfloat16 [64, 16, 4096], P('group', None, 'mp'), may hold values from -1.5 to 1.5
- request_adapter: int32 [16, 4], replicated, may hold values from 0 to 63
- adapter_row_index: int32 [64], replicated, may hold values from 0 to 63, each once
- request_token_length: int32 [16, 4], replicated, may hold values from 1 to 256, 512 in all within a row
- continues_previous: int32 [16], replicated, may hold values from 0 to 1, as said below
- request_cache_block: int32 [16, 4], replicated, may hold values from 0 to 31, as said below
- cached_length: int32 [16, 4], replicated, may hold values from 1 to 256
- cached_rotated_keys: bfloat16 [32, 256, 2048], P('group', None, 'mp'), may hold values from -6 to 6
- cached_value_rows: bfloat16 [32, 256, 2048], P('group', None, 'mp'), may hold values from -6 to 6
Outputs:
- attn_out: bfloat16 [8192, 3584], P('group', 'mp')
Inputs may be any that keep to these rules, and one draw needn't show every extreme that they name: `continues_previous`: the first group has 0; some group has 1. `request_cache_block`: the owner of block b is group b // 2; blocks may be shared by requests.
All inputs are finite; a program needn't handle non-finite values.
Results may differ from a plain program's by a relative error of at most 0.017.
The roundings to bfloat16 on the way count: a program that leaves them out, or rounds other values in their place, can miss the bound.
Values may be sent and summed in bfloat16 or wider, within the bound.
No kernel may reach another device: no remote copies, remote signals or barrier semaphores. Data moves between devices by JAX's collectives and lax.ppermute only.
A program may use at most 128 MiB of HBM per device.

v0:
```python
import jax
import jax.numpy as jnp
from jax import lax
from jax.sharding import PartitionSpec as P

HEAD_WIDTH = 256
REQS = 4
adapter_scale = 2.0


def shifted(value, axis, steps):
    count = lax.axis_size(axis)
    first, last = (max(0, -steps), min(count, count - steps))
    return lax.ppermute(value, axis, [(source, source + steps) for source in range(first, last)])


def rotate(values, position, head_size):
    count = values.shape[0]
    shaped = values.reshape(count, -1, head_size)
    half = head_size // 2
    freq = 10000.0 ** (-jnp.arange(half, dtype=jnp.float32) / half)
    angle = position[:, None, None] * freq[None, None, :]
    cosine = jnp.cos(angle)
    sine = jnp.sin(angle)
    first = shaped[..., :half]
    second = shaped[..., half:]
    turned = jnp.concatenate(
        [first * cosine - second * sine, second * cosine + first * sine], axis=-1
    )
    return turned.reshape(count, -1)


def layout(lengths, cached, split_flag, prev_len, count):
    ends = jnp.cumsum(lengths)
    starts = ends - lengths
    place = jnp.arange(count, dtype=jnp.int32)
    member = ((place[:, None] >= starts[None, :]) & (place[:, None] < ends[None, :])).astype(
        jnp.int32
    )
    request = jnp.sum(member * jnp.arange(lengths.shape[0], dtype=jnp.int32)[None, :], axis=1)
    offset = place - jnp.sum(member * starts[None, :], axis=1)
    extra = jnp.where(request == 0, split_flag * prev_len, 0)
    position = jnp.sum(member * cached[None, :], axis=1) + extra + offset
    return (member, request, position.astype(jnp.float32))


def attend(
    query_vectors,
    keys,
    values,
    prev_keys,
    prev_values,
    cache_keys,
    cache_values,
    request,
    cached,
    split_flag,
    prev_len,
    head_size,
):
    count = query_vectors.shape[0]
    kv_heads = keys.shape[1] // head_size
    ratio = query_vectors.shape[1] // keys.shape[1]
    block = cache_keys.shape[1]
    slots = cache_keys.shape[0] * block
    every_key = jnp.concatenate([cache_keys.reshape(slots, -1), prev_keys, keys], 0).reshape(
        -1, kv_heads, head_size
    )
    every_value = jnp.concatenate(
        [cache_values.reshape(slots, -1), prev_values, values], 0
    ).reshape(-1, kv_heads, head_size)
    slot_req = jnp.arange(slots, dtype=jnp.int32) // block
    slot_col = jnp.arange(slots, dtype=jnp.int32) % block
    cache_ok = (request[:, None] == slot_req[None, :]) & (
        slot_col[None, :] < cached[slot_req][None, :]
    )
    place = jnp.arange(count, dtype=jnp.int32)
    prev_ok = (split_flag == 1) & (request[:, None] == 0) & (place[None, :] >= count - prev_len)
    own_ok = (request[:, None] == request[None, :]) & (place[None, :] <= place[:, None])
    allowed = jnp.concatenate([cache_ok, prev_ok, own_ok], 1)
    grouped = query_vectors.reshape(count, kv_heads, ratio, head_size)
    scores = jnp.einsum(
        "tkrd,skd->krts", grouped, every_key, preferred_element_type=jnp.float32
    ) * head_size ** (-0.5)
    scores = jnp.where(allowed[None, None], scores, jnp.float32(-1e30))
    top = jnp.max(scores, axis=-1, keepdims=True)
    weights = jnp.exp(scores - top)
    total = jnp.sum(weights, axis=-1)
    numer = jnp.einsum(
        "krts,skd->tkrd",
        weights.astype(jnp.bfloat16),
        every_value,
        preferred_element_type=jnp.float32,
    )
    result = numer / jnp.transpose(total, (2, 0, 1))[..., None]
    return result.reshape(count, -1).astype(jnp.bfloat16)


def on_device(
    stream,
    prenorm_gain,
    query_weight,
    key_weight,
    value_weight,
    output_weight,
    adapter_down_rows,
    adapter_up_query,
    request_adapter,
    adapter_row_index,
    request_token_length,
    continues_previous,
    request_cache_block,
    cached_length,
    cached_rotated_keys,
    cached_value_rows,
):
    count = stream.shape[0]
    width = stream.shape[1]
    group_at = lax.axis_index("group")
    model_at = lax.axis_index("mp")
    whole = lax.all_gather(stream, "mp", axis=1, tiled=True)
    wide = whole.astype(jnp.float32)
    normalized_input = (
        wide * lax.rsqrt(jnp.mean(wide * wide, axis=1, keepdims=True) + 1e-06) * prenorm_gain
    ).astype(jnp.bfloat16)
    normed_part = lax.dynamic_slice_in_dim(normalized_input, model_at * width, width, 1)
    before = jnp.maximum(group_at - 1, 0)
    lengths = request_token_length[group_at]
    cached = cached_length[group_at]
    split_flag = continues_previous[group_at]
    prev_len = request_token_length[before, REQS - 1]
    member, request, position = layout(lengths, cached, split_flag, prev_len, count)
    wanted = adapter_row_index[request_adapter[group_at]]
    pieces = (
        lax.all_gather(adapter_down_rows, "group", axis=0, tiled=True),
        lax.all_gather(adapter_up_query, "group", axis=0, tiled=True),
    )
    stored = jnp.arange(pieces[0].shape[0], dtype=jnp.int32)
    onehot = (wanted[:, None] == stored[None, :]).astype(jnp.bfloat16)
    new_down = jnp.einsum("rj,jkd->rkd", onehot, pieces[0], preferred_element_type=jnp.float32)
    new_up = jnp.einsum("rj,jkd->rkd", onehot, pieces[1], preferred_element_type=jnp.float32)
    chosen_down = new_down.astype(jnp.bfloat16)
    chosen_up = new_up.astype(jnp.bfloat16)
    rank_index = adapter_down_rows.shape[1]
    partial_low = jnp.einsum(
        "td,rkd->trk", normed_part, chosen_down, preferred_element_type=jnp.float32
    ).reshape(count, REQS * rank_index)
    low = lax.psum(partial_low, "mp").astype(jnp.bfloat16)
    own_columns = jnp.repeat(member, rank_index, axis=1).astype(jnp.bfloat16)
    query_update = jnp.dot(
        low * own_columns,
        chosen_up.reshape(REQS * rank_index, -1),
        preferred_element_type=jnp.float32,
    )
    query_vectors = (
        jnp.dot(normalized_input, query_weight, preferred_element_type=jnp.float32)
        + adapter_scale * query_update
    )
    query_vectors = rotate(query_vectors, position, HEAD_WIDTH).astype(jnp.bfloat16)
    keys = rotate(
        jnp.dot(normalized_input, key_weight, preferred_element_type=jnp.float32),
        position,
        HEAD_WIDTH,
    ).astype(jnp.bfloat16)
    values = jnp.dot(normalized_input, value_weight, preferred_element_type=jnp.float32).astype(
        jnp.bfloat16
    )
    prev_keys, prev_values = shifted((keys, values), "group", 1)
    blocks = request_cache_block[group_at]
    pieces = (
        lax.all_gather(cached_rotated_keys, "group", axis=0, tiled=True),
        lax.all_gather(cached_value_rows, "group", axis=0, tiled=True),
    )
    stored = jnp.arange(pieces[0].shape[0], dtype=jnp.int32)
    onehot = (blocks[:, None] == stored[None, :]).astype(jnp.bfloat16)
    new_keys = jnp.einsum("rj,jcd->rcd", onehot, pieces[0], preferred_element_type=jnp.float32)
    new_values = jnp.einsum("rj,jcd->rcd", onehot, pieces[1], preferred_element_type=jnp.float32)
    cache_keys = new_keys.astype(jnp.bfloat16)
    cache_values = new_values.astype(jnp.bfloat16)
    attended = attend(
        query_vectors,
        keys,
        values,
        prev_keys,
        prev_values,
        cache_keys,
        cache_values,
        request,
        cached,
        split_flag,
        prev_len,
        HEAD_WIDTH,
    )
    partial_out = jnp.dot(attended, output_weight, preferred_element_type=jnp.float32)
    return lax.psum_scatter(partial_out.astype(jnp.bfloat16), "mp", scatter_dimension=1, tiled=True)


def solution(mesh):
    placed = (
        P("group", "mp"),
        P(),
        P(None, "mp"),
        P(None, "mp"),
        P(None, "mp"),
        P("mp", None),
        P("group", None, "mp"),
        P("group", None, "mp"),
        P(),
        P(),
        P(),
        P(),
        P(),
        P(),
        P("group", None, "mp"),
        P("group", None, "mp"),
    )
    return jax.shard_map(
        on_device, mesh=mesh, in_specs=placed, out_specs=P("group", "mp"), check_vma=False
    )
```

profile of v0, /device:TPU:0, one launch (start us, length us, event | category | flops | bytes accessed | tf_op | source)
XLA Modules:
  0.0 254.0 jit_solution(16617972660007501374)
XLA Ops:
  6.5 0.7 all-gather.11.cloned.1.call-update
  7.3 0.7 all-gather.7.cloned.1.call-update
  8.1 0.7 all-gather.5.cloned.1.call-update
  8.8 0.5 all-gather.9.cloned.1.call-update
  9.4 1.3 constant_dynamic-slice_fusion.2
  10.7 0.9 dynamic-slice_reduce_fusion
  11.9 0.9 fusion.79
  12.8 0.6 fusion.81
  13.4 26.9 %all_gather.18 = bf16[64,16,448]{2,1,0:T(8,128)(2,1)S(1)} all-gather(bf16[4,16,448]{2,1,0:T(8,128)(2,1)} %param.22), channel_id=1, replica_groups=mesh['group'=16,'mp'=8] {'group'}, dimensions={0}, use_global_device_ids=true | all-gather | bytes 974848 | tf_op jit(solution)/shard_map/all_gather | solution.py:135
  40.9 2.6 %compare_select_fusion.1 = s32[1024,1]{0,1:T(1,128)S(1)} fusion(s32[]{:T(128)} %bitcast.7, s32[]{:T(128)} %bitcast.8, s32[]{:T(128)} %bitcast.10, s32[]{:T(128)} %bitcast.9), kind=kLoop, calls=%fused_computation.71 | loop fusion | flops 17408 | bytes 4112 | tf_op jit(solution)/shard_map/gather | solution.py:75
  43.5 1.2 dynamic_slice.24
  46.8 0.9 dynamic-slice_reduce_fusion.1
  47.6 1.3 gather_fusion
  49.5 1.8 multiply_cosine_fusion
  51.4 0.8 compare_and_fusion
  52.2 1.2 convolution_convert_fusion.3
  53.8 1.2 all-gather.11.cloned.1.call-done
  54.9 2.4 convolution_convert_fusion.2
  57.4 28.5 %all-gather.7.cloned.1.call-done = bf16[512,3584]{0,1:T(8,128)(2,1)} async-done(((bf16[512,448]{0,1:T(8,128)(2,1)}), bf16[512,3584]{0,1:T(8,128)(2,1)}) %all-gather.7.cloned.1.call-update) | async-done | bytes 3670032 | tf_op jit(solution)/shard_map/all_gather | solution.py:121
  85.8 3.0 %fusion.2 = f32[512]{0:T(512)S(1)} fusion(bf16[512,3584]{0,1:T(8,128)(2,1)} %all-gather.7.cloned.1.call-done), kind=kLoop, calls=%fused_computation.7 | loop fusion | flops 5504512 | bytes 3672064 | tf_op jit(solution)/shard_map/reduce_sum | solution.py:124
  89.0 1.6 fusion.4
  90.6 1.8 copy-done.2
  92.4 1.9 convolution_convert_fusion.1
  94.3 1.8 copy.47
  96.1 4.2 %collective-permute-start = (bf16[512,256]{1,0:T(8,128)(2,1)}, bf16[512,256]{1,0:T(8,128)(2,1)}, u32[]{:S(2)}, u32[]{:S(2)}) collective-permute-start(bf16[512,256]{1,0:T(8,128)(2,1)} %convolution_convert_fusion.1), channel_id=1, source_target_pairs={{0,8},{8,16},{16,24},{24,32},{32,40},{40,48},{48,56},{56,64},{64,7... | collective-permute-start | bytes 786440 | tf_op jit(solution)/shard_map/ppermute | solution.py:14
  100.2 3.8 %convolution_bitcast_fusion = f32[512,1,256]{0,2,1:T(8,128)S(1)} fusion(bf16[512,3584]{0,1:T(8,128)(2,1)} %copy-done.2, bf16[3584,256]{1,0:T(8,128)(2,1)} %param.19), kind=kOutput, calls=%fused_computation.26 | convolution fusion | flops 939524096 | bytes 6029312 | tf_op jit(solution)/shard_map/dot_general | solution.py:161
  104.0 1.2 fusion.49
  105.2 0.7 maximum_bitcast_fusion.6
  105.9 1.8 copy.52
  107.7 3.4 %collective-permute-start.1 = (bf16[512,256]{0,1:T(8,128)(2,1)}, bf16[512,256]{0,1:T(8,128)(2,1)}, u32[]{:S(2)}, u32[]{:S(2)}) collective-permute-start(bf16[512,256]{0,1:T(8,128)(2,1)} %maximum_bitcast_fusion.6), channel_id=1, source_target_pairs={{0,8},{8,16},{16,24},{24,32},{32,40},{40,48},{48,56},{56,64},{64,7... | collective-permute-start | bytes 786440 | tf_op jit(solution)/shard_map/ppermute | solution.py:14
  111.1 1.2 fusion.41
  112.3 26.0 %all-reduce.1 = bf16[512,64]{0,1:T(8,128)(2,1)S(1)} all-reduce(f32[512,64]{0,1:T(8,128)S(1)} %bitcast.101), channel_id=1, replica_groups=mesh['group'=16,'mp'=8] {'mp'}, use_global_device_ids=true, to_apply=%region_5.6 | all-reduce | flops 32768 | bytes 196608 | tf_op jit(solution)/shard_map/psum | solution.py:148
  138.4 5.3 %fusion.82 = f32[512,512]{0,1:T(8,128)S(1)} fusion(bf16[512,3584]{0,1:T(8,128)(2,1)} %copy-done.2, bf16[3584,512]{1,0:T(8,128)(2,1)} %param.18), kind=kOutput, calls=%fused_computation.129 | convolution fusion | flops 1879048192 | bytes 8388608 | tf_op jit(solution)/shard_map/dot_general | solution.py:156
  144.0 1.1 fusion.80
  145.1 1.2 copy.63
  146.4 2.1 copy.62
  148.5 2.2 subtract_convert_fusion
  150.6 1.8 copy.46
  152.5 1.8 copy.51
  154.3 4.6 %fusion.18 = bf16[4,256,256]{2,0,1:T(4,128)(2,1)S(1)} fusion(bf16[32,256,256]{2,1,0:T(8,128)(2,1)} %all-gather.5.cloned.1.call-done, s32[4]{0:T(128)S(1)} %dynamic-slice_reduce_fusion.1), kind=kOutput, calls=%fused_computation.24 | convolution fusion | flops 17039488 | bytes 4718608 | tf_op jit(solution)/shard_map/rj,jcd->rcd/dot_general | solution.py:177
  159.0 1.0 copy.45
  160.0 35.3 %all-gather.9.cloned.1.call-done = bf16[32,256,256]{2,1,0:T(8,128)(2,1)} async-done(((bf16[2,256,256]{2,1,0:T(8,128)(2,1)}), bf16[32,256,256]{2,1,0:T(8,128)(2,1)}) %all-gather.9.cloned.1.call-update) | async-done | bytes 4194320 | tf_op jit(solution)/shard_map/all_gather | solution.py:171
  195.3 4.7 %fusion.21 = bf16[4,256,256]{2,0,1:T(4,128)(2,1)S(1)} fusion(bf16[32,256,256]{2,1,0:T(8,128)(2,1)} %all-gather.9.cloned.1.call-done, s32[4]{0:T(128)S(1)} %dynamic-slice_reduce_fusion.1), kind=kOutput, calls=%fused_computation.25 | convolution fusion | flops 17039488 | bytes 4718608 | tf_op jit(solution)/shard_map/rj,jcd->rcd/dot_general | solution.py:176
  200.1 1.8 fusion.5
  201.9 2.2 fusion
  204.2 2.8 %divide_convert_fusion = bf16[512,1,2,256]{0,3,2,1:T(8,128)(2,1)S(1)} fusion(f32[2048,512,2]{1,0,2:T(8,128)S(1)} %get-tuple-element.25, f32[2,512]{1,0:T(2,128)S(1)} %get-tuple-element.24, pred[512,2048]{0,1:T(8,128)(4,1)S(1)} %pad_add_fusion, bf16[512,256]{0,1:T(8,128)(2,1)S(1)} %copy-done.4, bf16[512,256]{0,1:T(8,128)(2,1)S(1)} %copy-done.6, ...), kind=kOutput, calls=%fused_computation.43 | convolution fusion | flops 1085800448 | bytes 11018240 | tf_op jit(solution)/shard_map/krts,skd->tkrd/dot_general | solution.py:89
  207.0 3.9 %convolution_convert_fusion = bf16[512,3584]{0,1:T(8,128)(2,1)} fusion(bf16[512,512]{0,1:T(8,128)(2,1)S(1)} %bitcast.107, bf16[512,3584]{1,0:T(8,128)(2,1)S(1)} %copy-done.11), kind=kOutput, calls=%fused_computation.11 | convolution fusion | flops 1880883200 | bytes 7864320 | tf_op jit(solution)/shard_map/dot_general | solution.py:194
  210.9 36.5 %reduce-scatter.2.cloned.1.call-done = bf16[512,448]{0,1:T(8,128)(2,1)} async-done(((bf16[512,3584]{0,1:T(8,128)(2,1)}), bf16[512,448]{0,1:T(8,128)(2,1)}) %reduce-scatter.2.cloned.1.call-update) | async-done | bytes 458768 | tf_op jit(solution)/shard_map/reduce_scatter | solution.py:195
  (54 shorter events, 2.1 us)
Async XLA Ops:
  6.5 85.8 %copy-start = (bf16[3584,256]{1,0:T(8,128)(2,1)S(1)}, bf16[3584,256]{1,0:T(8,128)(2,1)}, u32[]{:S(2)}) copy-start(bf16[3584,256]{1,0:T(8,128)(2,1)} %param.20) | copy-start | bytes 5505028
  6.5 48.4 %all-gather.11.cloned.1.call-start = ((), (), s32[]{:S(2)}) async-start(), calls=%async_computation.4 | async-start | bytes 1114112 | tf_op jit(solution)/shard_map/all_gather | solution.py:136
  7.3 78.6 %all-gather.7.cloned.1.call-start = ((), (), s32[]{:S(2)}) async-start(), calls=%async_computation.2 | async-start | bytes 4128768 | tf_op jit(solution)/shard_map/all_gather | solution.py:121
  8.0 146.3 %all-gather.5.cloned.1.call-start = ((), (), s32[]{:S(2)}) async-start(), calls=%async_computation.1 | async-start | bytes 4456448 | tf_op jit(solution)/shard_map/all_gather | solution.py:172
  8.7 186.5 %all-gather.9.cloned.1.call-start = ((), (), s32[]{:S(2)}) async-start(), calls=%async_computation.3 | async-start | bytes 4456448 | tf_op jit(solution)/shard_map/all_gather | solution.py:171
  9.3 238.1 %reduce-scatter.2.cloned.1.call-start = ((), (), s32[]{:S(2)}) async-start(), calls=%async_computation.5 | async-start | bytes 4128768 | tf_op jit(solution)/shard_map/reduce_scatter | solution.py:195
  53.4 35.5 %copy-start.10 = (f32[3584]{0:T(1024)S(1)}, f32[3584]{0:T(1024)}, u32[]{:S(2)}) copy-start(f32[3584]{0:T(1024)} %param.17) | copy-start | bytes 43012
  85.8 3.1 %copy-start.1 = (bf16[512,3584]{0,1:T(8,128)(2,1)S(1)}, bf16[512,3584]{0,1:T(8,128)(2,1)}, u32[]{:S(2)}) copy-start(bf16[512,3584]{0,1:T(8,128)(2,1)} %all-gather.7.cloned.1.call-done) | copy-start | bytes 11010052
  90.5 1.8 copy-start.2
  96.1 54.6 %collective-permute-start = (bf16[512,256]{1,0:T(8,128)(2,1)}, bf16[512,256]{1,0:T(8,128)(2,1)}, u32[]{:S(2)}, u32[]{:S(2)}) collective-permute-start(bf16[512,256]{1,0:T(8,128)(2,1)} %convolution_convert_fusion.1), channel_id=1, source_target_pairs={{0,8},{8,16},{16,24},{24,32},{32,40},{40,48},{48,56},{56,64},{64,7... | collective-permute-start | bytes 786440 | tf_op jit(solution)/shard_map/ppermute | solution.py:14
  107.7 44.8 %collective-permute-start.1 = (bf16[512,256]{0,1:T(8,128)(2,1)}, bf16[512,256]{0,1:T(8,128)(2,1)}, u32[]{:S(2)}, u32[]{:S(2)}) collective-permute-start(bf16[512,256]{0,1:T(8,128)(2,1)} %maximum_bitcast_fusion.6), channel_id=1, source_target_pairs={{0,8},{8,16},{16,24},{24,32},{32,40},{40,48},{48,56},{56,64},{64,7... | collective-permute-start | bytes 786440 | tf_op jit(solution)/shard_map/ppermute | solution.py:14
  160.0 40.1 %copy-start.5 = (bf16[512,256]{1,0:T(8,128)(2,1)S(1)}, bf16[512,256]{1,0:T(8,128)(2,1)}, u32[]{:S(2)}) copy-start(bf16[512,256]{1,0:T(8,128)(2,1)} %copy.52) | copy-start | bytes 786436
  160.0 40.1 %copy-start.7 = (bf16[512,256]{1,0:T(8,128)(2,1)S(1)}, bf16[512,256]{1,0:T(8,128)(2,1)}, u32[]{:S(2)}) copy-start(bf16[512,256]{1,0:T(8,128)(2,1)} %copy.51) | copy-start | bytes 786436
  195.3 4.8 %copy-start.8 = (bf16[512,2,128]{2,0,1:T(8,128)(2,1)S(1)}, bf16[512,2,128]{2,0,1:T(8,128)(2,1)}, u32[]{:S(2)}) copy-start(bf16[512,2,128]{2,0,1:T(8,128)(2,1)} %get-tuple-element.12) | copy-start | bytes 786436
  195.3 4.8 %copy-start.9 = (bf16[512,2,128]{2,0,1:T(8,128)(2,1)S(1)}, bf16[512,2,128]{2,0,1:T(8,128)(2,1)}, u32[]{:S(2)}) copy-start(bf16[512,2,128]{2,0,1:T(8,128)(2,1)} %get-tuple-element.13) | copy-start | bytes 786436
  201.9 2.2 copy-start.3
  201.9 2.2 copy-start.4
  201.9 2.2 copy-start.6
  204.2 2.8 %copy-start.11 = (bf16[512,3584]{1,0:T(8,128)(2,1)S(1)}, bf16[512,3584]{1,0:T(8,128)(2,1)}, u32[]{:S(2)}) copy-start(bf16[512,3584]{1,0:T(8,128)(2,1)} %param.21) | copy-start | bytes 11010052
Sparse Core Ops, SparseCore 0:
  9.5 45.3 all-gather.10
  56.6 29.1 all-gather.6
  88.0 53.9 all-gather.4
  144.0 51.2 all-gather.8
  211.0 36.3 reduce-scatter.1
where the time goes:
time: 255 us; the launch traced here: 254 us
  waiting for transfers between devices  104 us (41%)
  blocking collectives  52.9 us (21%)
  matrix products  33.9 us (13%)
  local copies, waits for them, and re-layouts  21.9 us (9%)
  other arithmetic  17.3 us (7%)
  between operations  16.1 us (6%)
  starting transfers between devices  7.77 us (3%)
    reduce_scatter x1, waiting for transfers between devices, on_device(): lax.psum_scatter(partial_out.astype(jnp.bfloat16), 'mp', scatter_dimensio...  36.5 us
    all_gather x1, waiting for transfers between devices, on_device(): lax.all_gather(cached_rotated_keys, 'group', axis=0, tiled=True)  35.3 us
    all_gather x1, waiting for transfers between devices, on_device(): whole = lax.all_gather(stream, 'mp', axis=1, tiled=True)  28.5 us
    all_gather x1, blocking collectives, on_device(): lax.all_gather(adapter_down_rows, 'group', axis=0, tiled=True)  26.9 us
    psum x1, blocking collectives, on_device(): low = lax.psum(partial_low, 'mp').astype(jnp.bfloat16)  26 us
    ppermute x2, starting transfers between devices, shifted(): lax.ppermute(value, axis, [(source, source + steps) for source in range(f...  7.62 us
    unnamed x27, local copies, waits for them, and re-layouts  5.37 us
    dot_general x1, matrix products, on_device(): jnp.dot(normalized_input, query_weight, preferred_element_type=jnp.float32)  5.26 us
  transfers between devices with their start and end apart: 7, of which 4 were waited for; matrix products, arithmetic and copies ran while one was open for 22% of the time, Pallas kernels for 0%

commit v1 on v0

--- a/solution.py
+++ b/solution.py
@@ -132,7 +132,10 @@
     member, request, position = layout(lengths, cached, split_flag, prev_len, count)
     wanted = adapter_row_index[request_adapter[group_at]]
     pieces = (
-        lax.all_gather(adapter_down_rows, "group", axis=0, tiled=True),
+        jnp.concatenate(
+            lax.all_to_all(jnp.stack([adapter_down_rows] * lax.axis_size("group")), "group", 0, 0),
+            axis=0,
+        ),
         lax.all_gather(adapter_up_query, "group", axis=0, tiled=True),
     )
     stored = jnp.arange(pieces[0].shape[0], dtype=jnp.int32)

time: 255 us -> 259 us (1.016)
  waiting for transfers between devices: 104 us -> 131 us
  blocking collectives: 52.9 us -> 26 us
  starting transfers between devices: 7.77 us -> 15.8 us
  local copies, waits for them, and re-layouts: 21.9 us -> 19.2 us
    all_gather x1 -> x0, blocking collectives: 26.9 us -> none  [on_device(): lax.all_gather(adapter_down_rows, 'group', axis=0, tiled=True)]
    all_gather x1, waiting for transfers between devices: 1.16 us -> 18.6 us  [on_device(): lax.all_gather(adapter_up_query, 'group', axis=0, tiled=True)]
    all_to_all x0 -> x1, starting transfers between devices: none -> 7.96 us  [on_device(): lax.all_to_all(jnp.stack([adapter_down_rows] * lax.axis_size('group')), '...]
    all_to_all x0 -> x1, waiting for transfers between devices: none -> 4.8 us  [on_device(): lax.all_to_all(jnp.stack([adapter_down_rows] * lax.axis_size('group')), '...]
    all_gather x1, waiting for transfers between devices: 35.3 us -> 39.5 us  [on_device(): lax.all_gather(cached_rotated_keys, 'group', axis=0, tiled=True)]
    unnamed x27 -> x42, local copies, waits for them, and re-layouts: 5.37 us -> 3.33 us
  transfers between devices with their start and end apart: 7 -> 8, of which waited for: 4 -> 5; matrix products, arithmetic and copies ran while one was open for 22% -> 20% of each run, Pallas kernels for 0% -> 0%
where the time goes in v1:
time: 259 us
  waiting for transfers between devices  131 us (51%)
  matrix products  33.1 us (13%)
  blocking collectives  26 us (10%)
  local copies, waits for them, and re-layouts  19.2 us (7%)
  other arithmetic  18 us (7%)
  between operations  16.1 us (6%)
  starting transfers between devices  15.8 us (6%)
    all_gather x1, waiting for transfers between devices, on_device(): lax.all_gather(cached_rotated_keys, 'group', axis=0, tiled=True)  39.5 us
    reduce_scatter x1, waiting for transfers between devices, on_device(): lax.psum_scatter(partial_out.astype(jnp.bfloat16), 'mp', scatter_dimensio...  36.6 us
    all_gather x1, waiting for transfers between devices, on_device(): whole = lax.all_gather(stream, 'mp', axis=1, tiled=True)  28.5 us
    psum x1, blocking collectives, on_device(): low = lax.psum(partial_low, 'mp').astype(jnp.bfloat16)  26 us
    all_gather x1, waiting for transfers between devices, on_device(): lax.all_gather(adapter_up_query, 'group', axis=0, tiled=True)  18.6 us
    all_to_all x1, starting transfers between devices, on_device(): lax.all_to_all(jnp.stack([adapter_down_rows] * lax.axis_size('group')), '...  7.96 us
    ppermute x2, starting transfers between devices, shifted(): lax.ppermute(value, axis, [(source, source + steps) for source in range(f...  7.61 us
    dot_general x1, matrix products, on_device(): jnp.dot(normalized_input, query_weight, preferred_element_type=jnp.float32)  5.26 us
  transfers between devices with their start and end apart: 8, of which 5 were waited for; matrix products, arithmetic and copies ran while one was open for 20% of the time, Pallas kernels for 0%

profile of v1, /device:TPU:0, one launch (start us, length us, event | category | flops | bytes accessed | tf_op | source)
XLA Modules:
  0.0 258.8 jit_solution(3310667771535436416)
XLA Ops:
  6.6 0.7 all-gather.11.cloned.1.call-update
  7.3 0.7 all-gather.7.cloned.1.call-update
  8.1 0.7 all-gather.5.cloned.1.call-update
  8.8 0.9 copy.70
  9.7 1.4 stack.2
  11.1 8.0 %all-to-all-start = ((bf16[16,4,16,448]{3,1,2,0:T(4,128)(2,1)}), bf16[16,4,16,448]{3,1,2,0:T(4,128)(2,1)S(1)}, u32[]{:S(2)}, u32[]{:S(2)}) async-start(bf16[16,4,16,448]{3,1,2,0:T(4,128)(2,1)} %stack.2), calls=%async_computation | async-start | bytes 2097152 | tf_op jit(solution)/shard_map/all_to_all | solution.py:136
  19.1 0.5 all-gather.9.cloned.1.call-update
  19.7 0.6 constant_dynamic-slice_fusion.2
  21.0 0.6 fusion.80
  22.3 2.5 compare_select_fusion.1
  24.8 0.6 dynamic_slice.24
  27.5 0.6 gather_fusion
  28.7 1.8 multiply_cosine_fusion
  30.5 0.8 compare_and_fusion
  31.3 1.4 pad_add_fusion
  32.7 4.8 %all-to-all-done = bf16[16,4,16,448]{3,1,2,0:T(4,128)(2,1)S(1)} async-done(((bf16[16,4,16,448]{3,1,2,0:T(4,128)(2,1)}), bf16[16,4,16,448]{3,1,2,0:T(4,128)(2,1)S(1)}, u32[]{:S(2)}, u32[]{:S(2)}) %all-to-all-start) | async-done | bytes 917536 | tf_op jit(solution)/shard_map/all_to_all | solution.py:136
  37.5 1.5 copy.71
  39.0 1.6 reshape.319
  40.9 18.6 %all-gather.11.cloned.1.call-done = bf16[64,16,512]{2,1,0:T(8,128)(2,1)} async-done(((bf16[4,16,512]{2,1,0:T(8,128)(2,1)}), bf16[64,16,512]{2,1,0:T(8,128)(2,1)}) %all-gather.11.cloned.1.call-update) | async-done | bytes 1048592 | tf_op jit(solution)/shard_map/all_gather | solution.py:139
  59.5 2.4 convolution_convert_fusion.2
  62.0 28.5 %all-gather.7.cloned.1.call-done = bf16[512,3584]{0,1:T(8,128)(2,1)} async-done(((bf16[512,448]{0,1:T(8,128)(2,1)}), bf16[512,3584]{0,1:T(8,128)(2,1)}) %all-gather.7.cloned.1.call-update) | async-done | bytes 3670032 | tf_op jit(solution)/shard_map/all_gather | solution.py:121
  90.5 3.0 %fusion.2 = f32[512]{0:T(512)S(1)} fusion(bf16[512,3584]{0,1:T(8,128)(2,1)} %all-gather.7.cloned.1.call-done), kind=kLoop, calls=%fused_computation.7 | loop fusion | flops 5504512 | bytes 3672064 | tf_op jit(solution)/shard_map/reduce_sum | solution.py:124
  93.6 1.6 fusion.4
  95.2 1.8 copy-done.4
  97.0 1.9 convolution_convert_fusion.1
  98.9 1.8 copy.64
  100.7 4.2 %collective-permute-start = (bf16[512,256]{1,0:T(8,128)(2,1)}, bf16[512,256]{1,0:T(8,128)(2,1)}, u32[]{:S(2)}, u32[]{:S(2)}) collective-permute-start(bf16[512,256]{1,0:T(8,128)(2,1)} %convolution_convert_fusion.1), channel_id=1, source_target_pairs={{0,8},{8,16},{16,24},{24,32},{32,40},{40,48},{48,56},{56,64},{64,7... | collective-permute-start | bytes 786440 | tf_op jit(solution)/shard_map/ppermute | solution.py:14
  104.9 3.8 %convolution_bitcast_fusion = f32[512,1,256]{0,2,1:T(8,128)S(1)} fusion(bf16[512,3584]{0,1:T(8,128)(2,1)} %copy-done.4, bf16[3584,256]{1,0:T(8,128)(2,1)} %param.19), kind=kOutput, calls=%fused_computation.26 | convolution fusion | flops 939524096 | bytes 6029312 | tf_op jit(solution)/shard_map/dot_general | solution.py:164
  108.6 1.2 fusion.48
  109.8 0.7 maximum_bitcast_fusion.6
  110.6 1.8 copy.69
  112.3 3.4 %collective-permute-start.1 = (bf16[512,256]{0,1:T(8,128)(2,1)}, bf16[512,256]{0,1:T(8,128)(2,1)}, u32[]{:S(2)}, u32[]{:S(2)}) collective-permute-start(bf16[512,256]{0,1:T(8,128)(2,1)} %maximum_bitcast_fusion.6), channel_id=1, source_target_pairs={{0,8},{8,16},{16,24},{24,32},{32,40},{40,48},{48,56},{56,64},{64,7... | collective-permute-start | bytes 786440 | tf_op jit(solution)/shard_map/ppermute | solution.py:14
  115.8 1.2 fusion.40
  117.0 26.0 %all-reduce.1 = bf16[512,64]{0,1:T(8,128)(2,1)S(1)} all-reduce(f32[512,64]{0,1:T(8,128)S(1)} %bitcast.104), channel_id=1, replica_groups=mesh['group'=16,'mp'=8] {'mp'}, use_global_device_ids=true, to_apply=%region_5.6 | all-reduce | flops 32768 | bytes 196608 | tf_op jit(solution)/shard_map/psum | solution.py:151
  143.1 5.3 %fusion.81 = f32[512,512]{0,1:T(8,128)S(1)} fusion(bf16[512,3584]{0,1:T(8,128)(2,1)} %copy-done.4, bf16[3584,512]{1,0:T(8,128)(2,1)} %param.18), kind=kOutput, calls=%fused_computation.128 | convolution fusion | flops 1879048192 | bytes 8388608 | tf_op jit(solution)/shard_map/dot_general | solution.py:159
  148.3 0.3 fusion.17
  149.2 2.0 subtract_convert_fusion
  151.1 1.8 copy.63
  152.9 1.8 copy.68
  154.7 4.6 %fusion.18 = bf16[4,256,256]{2,0,1:T(4,128)(2,1)S(1)} fusion(bf16[32,256,256]{2,1,0:T(8,128)(2,1)} %all-gather.5.cloned.1.call-done, s32[4]{0:T(128)S(1)} %dynamic-slice_reduce_fusion.1), kind=kOutput, calls=%fused_computation.24 | convolution fusion | flops 17039488 | bytes 4718608 | tf_op jit(solution)/shard_map/rj,jcd->rcd/dot_general | solution.py:180
  159.5 1.0 copy.62
  160.5 39.5 %all-gather.9.cloned.1.call-done = bf16[32,256,256]{2,1,0:T(8,128)(2,1)} async-done(((bf16[2,256,256]{2,1,0:T(8,128)(2,1)}), bf16[32,256,256]{2,1,0:T(8,128)(2,1)}) %all-gather.9.cloned.1.call-update) | async-done | bytes 4194320 | tf_op jit(solution)/shard_map/all_gather | solution.py:174
  200.0 4.7 %fusion.21 = bf16[4,256,256]{2,0,1:T(4,128)(2,1)S(1)} fusion(bf16[32,256,256]{2,1,0:T(8,128)(2,1)} %all-gather.9.cloned.1.call-done, s32[4]{0:T(128)S(1)} %dynamic-slice_reduce_fusion.1), kind=kOutput, calls=%fused_computation.25 | convolution fusion | flops 17039488 | bytes 4718608 | tf_op jit(solution)/shard_map/rj,jcd->rcd/dot_general | solution.py:179
  204.8 1.9 fusion.5
  206.7 2.2 fusion
  208.9 2.8 %divide_convert_fusion = bf16[512,1,2,256]{0,3,2,1:T(8,128)(2,1)S(1)} fusion(f32[2048,512,2]{1,0,2:T(8,128)S(1)} %get-tuple-element.25, f32[2,512]{1,0:T(2,128)S(1)} %get-tuple-element.24, pred[512,2048]{0,1:T(8,128)(4,1)S(1)} %copy-done.3, bf16[512,256]{0,1:T(8,128)(2,1)S(1)} %copy-done.6, bf16[512,256]{0,1:T(8,128)(2,1)S(1)} %copy-done.8, ...), kind=kOutput, calls=%fused_computation.42 | convolution fusion | flops 1085800448 | bytes 11018240 | tf_op jit(solution)/shard_map/krts,skd->tkrd/dot_general | solution.py:89
  211.7 3.9 %convolution_convert_fusion = bf16[512,3584]{0,1:T(8,128)(2,1)} fusion(bf16[512,512]{0,1:T(8,128)(2,1)S(1)} %bitcast.110, bf16[512,3584]{1,0:T(8,128)(2,1)S(1)} %copy-done.17), kind=kOutput, calls=%fused_computation.11 | convolution fusion | flops 1880883200 | bytes 7864320 | tf_op jit(solution)/shard_map/dot_general | solution.py:197
  215.7 36.6 %reduce-scatter.2.cloned.1.call-done = bf16[512,448]{0,1:T(8,128)(2,1)} async-done(((bf16[512,3584]{0,1:T(8,128)(2,1)}), bf16[512,448]{0,1:T(8,128)(2,1)}) %reduce-scatter.2.cloned.1.call-update) | async-done | bytes 458768 | tf_op jit(solution)/shard_map/reduce_scatter | solution.py:198
  (73 shorter events, 2.8 us)
Async XLA Ops:
  6.5 90.5 %copy-start = (bf16[3584,256]{1,0:T(8,128)(2,1)S(1)}, bf16[3584,256]{1,0:T(8,128)(2,1)}, u32[]{:S(2)}) copy-start(bf16[3584,256]{1,0:T(8,128)(2,1)} %param.20) | copy-start | bytes 5505028
  6.5 13.1 %copy-start.14 = (s32[16,4]{0,1:T(4,128)S(1)}, s32[16,4]{0,1:T(4,128)}, u32[]{:S(2)}) copy-start(s32[16,4]{0,1:T(4,128)} %param.26) | copy-start | bytes 772
  6.5 13.8 %copy-start.13 = (s32[16,4]{0,1:T(4,128)S(1)}, s32[16,4]{0,1:T(4,128)}, u32[]{:S(2)}) copy-start(s32[16,4]{0,1:T(4,128)} %param.24) | copy-start | bytes 772
  6.5 14.3 %copy-start.16 = (s32[16,4]{0,1:T(4,128)S(1)}, s32[16,4]{0,1:T(4,128)}, u32[]{:S(2)}) copy-start(s32[16,4]{0,1:T(4,128)} %param.29) | copy-start | bytes 772
  6.5 18.3 %copy-start.18 = (s32[16]{0:T(128)S(1)}, s32[16]{0:T(128)}, u32[]{:S(2)}) copy-start(s32[16]{0:T(128)} %param.27) | copy-start | bytes 196
  6.5 20.8 %copy-start.15 = (s32[16,4]{0,1:T(4,128)S(1)}, s32[16,4]{0,1:T(4,128)}, u32[]{:S(2)}) copy-start(s32[16,4]{0,1:T(4,128)} %param.28) | copy-start | bytes 772
  6.6 21.0 %copy-start.1 = (s32[64]{0:T(128)S(1)}, s32[64]{0:T(128)}, u32[]{:S(2)}) copy-start(s32[64]{0:T(128)} %param.25) | copy-start | bytes 772
  6.6 53.0 %all-gather.11.cloned.1.call-start = ((), (), s32[]{:S(2)}) async-start(), calls=%async_computation.5 | async-start | bytes 1114112 | tf_op jit(solution)/shard_map/all_gather | solution.py:139
  7.3 83.2 %all-gather.7.cloned.1.call-start = ((), (), s32[]{:S(2)}) async-start(), calls=%async_computation.3 | async-start | bytes 4128768 | tf_op jit(solution)/shard_map/all_gather | solution.py:121
  8.1 146.7 %all-gather.5.cloned.1.call-start = ((), (), s32[]{:S(2)}) async-start(), calls=%async_computation.2 | async-start | bytes 4456448 | tf_op jit(solution)/shard_map/all_gather | solution.py:175
  11.1 26.5 %all-to-all-start = ((bf16[16,4,16,448]{3,1,2,0:T(4,128)(2,1)}), bf16[16,4,16,448]{3,1,2,0:T(4,128)(2,1)S(1)}, u32[]{:S(2)}, u32[]{:S(2)}) async-start(bf16[16,4,16,448]{3,1,2,0:T(4,128)(2,1)} %stack.2), calls=%async_computation | async-start | bytes 2097152 | tf_op jit(solution)/shard_map/all_to_all | solution.py:136
  19.0 180.9 %all-gather.9.cloned.1.call-start = ((), (), s32[]{:S(2)}) async-start(), calls=%async_computation.4 | async-start | bytes 4456448 | tf_op jit(solution)/shard_map/all_gather | solution.py:174
  19.6 232.7 %reduce-scatter.2.cloned.1.call-start = ((), (), s32[]{:S(2)}) async-start(), calls=%async_computation.6 | async-start | bytes 4128768 | tf_op jit(solution)/shard_map/reduce_scatter | solution.py:198
  39.0 54.5 %copy-start.12 = (f32[3584]{0:T(1024)S(1)}, f32[3584]{0:T(1024)}, u32[]{:S(2)}) copy-start(f32[3584]{0:T(1024)} %param.17) | copy-start | bytes 43012
  90.5 3.1 %copy-start.2 = (bf16[512,3584]{0,1:T(8,128)(2,1)S(1)}, bf16[512,3584]{0,1:T(8,128)(2,1)}, u32[]{:S(2)}) copy-start(bf16[512,3584]{0,1:T(8,128)(2,1)} %all-gather.7.cloned.1.call-done) | copy-start | bytes 11010052
  95.2 1.8 copy-start.4
  100.7 50.4 %collective-permute-start = (bf16[512,256]{1,0:T(8,128)(2,1)}, bf16[512,256]{1,0:T(8,128)(2,1)}, u32[]{:S(2)}, u32[]{:S(2)}) collective-permute-start(bf16[512,256]{1,0:T(8,128)(2,1)} %convolution_convert_fusion.1), channel_id=1, source_target_pairs={{0,8},{8,16},{16,24},{24,32},{32,40},{40,48},{48,56},{56,64},{64,7... | collective-permute-start | bytes 786440 | tf_op jit(solution)/shard_map/ppermute | solution.py:14
  112.3 40.6 %collective-permute-start.1 = (bf16[512,256]{0,1:T(8,128)(2,1)}, bf16[512,256]{0,1:T(8,128)(2,1)}, u32[]{:S(2)}, u32[]{:S(2)}) collective-permute-start(bf16[512,256]{0,1:T(8,128)(2,1)} %maximum_bitcast_fusion.6), channel_id=1, source_target_pairs={{0,8},{8,16},{16,24},{24,32},{32,40},{40,48},{48,56},{56,64},{64,7... | collective-permute-start | bytes 786440 | tf_op jit(solution)/shard_map/ppermute | solution.py:14
  159.4 45.3 %copy-start.3 = (pred[512,2048]{0,1:T(8,128)(4,1)S(1)}, pred[512,2048]{0,1:T(8,128)(4,1)}, u32[]{:S(2)}) copy-start(pred[512,2048]{0,1:T(8,128)(4,1)} %pad_add_fusion) | copy-start | bytes 3145732
  160.5 44.2 %copy-start.7 = (bf16[512,256]{1,0:T(8,128)(2,1)S(1)}, bf16[512,256]{1,0:T(8,128)(2,1)}, u32[]{:S(2)}) copy-start(bf16[512,256]{1,0:T(8,128)(2,1)} %copy.69) | copy-start | bytes 786436
  160.5 44.3 %copy-start.9 = (bf16[512,256]{1,0:T(8,128)(2,1)S(1)}, bf16[512,256]{1,0:T(8,128)(2,1)}, u32[]{:S(2)}) copy-start(bf16[512,256]{1,0:T(8,128)(2,1)} %copy.68) | copy-start | bytes 786436
  200.0 4.8 %copy-start.10 = (bf16[512,2,128]{2,0,1:T(8,128)(2,1)S(1)}, bf16[512,2,128]{2,0,1:T(8,128)(2,1)}, u32[]{:S(2)}) copy-start(bf16[512,2,128]{2,0,1:T(8,128)(2,1)} %get-tuple-element.12) | copy-start | bytes 786436
  200.0 4.8 %copy-start.11 = (bf16[512,2,128]{2,0,1:T(8,128)(2,1)S(1)}, bf16[512,2,128]{2,0,1:T(8,128)(2,1)}, u32[]{:S(2)}) copy-start(bf16[512,2,128]{2,0,1:T(8,128)(2,1)} %get-tuple-element.13) | copy-start | bytes 786436
  206.6 2.2 copy-start.5
  206.6 2.2 copy-start.6
  206.7 2.2 copy-start.8
  208.9 2.8 %copy-start.17 = (bf16[512,3584]{1,0:T(8,128)(2,1)S(1)}, bf16[512,3584]{1,0:T(8,128)(2,1)}, u32[]{:S(2)}) copy-start(bf16[512,3584]{1,0:T(8,128)(2,1)} %param.21) | copy-start | bytes 11010052
Sparse Core Ops, SparseCore 0:
  9.5 49.9 all-gather.10
  61.2 29.2 all-gather.6
  92.6 53.9 all-gather.4
  148.7 51.2 all-gather.8
  215.8 36.4 reduce-scatter.1
